TPU v7x, 32 devices: a whole 2x2x4 slice. The times are simulated.
32 devices in a mesh: freq: 4 (over y, core), row: 8 (over z, x).
Axes of the slice: x: 2, y: 2, z: 4, core: 2. Of those that a mesh axis runs over, the one named last changes fastest.
Arguments:
- traces: bfloat16 [2, 8192, 8192], P(None, ('freq', 'row')), may hold values from -1.1953125 to 1.1953125
- prior: bfloat16 [4, 2, 8192, 8192], P('freq', None, None, 'row'), may hold values from -0.796875 to 0.796875
- bins: int32 [4], replicated, may hold values from 64 to 255
- panels: int32 [2], replicated, may hold values from 0 to 31
Outputs:
- multiples: bfloat16 [4, 2, 8192, 8192], P('freq', None, 'row')
- spectrum: bfloat16 [4, 2, 8192, 8192], P('freq', None, None, 'row')
All inputs are finite; a program needn't handle non-finite values.
Results may differ from a plain program's by a relative error of at most 0.0077.
Values may be sent and summed in bfloat16 or wider, within the bound.
No kernel may reach another device: no remote copies, remote signals or barrier semaphores. Data moves between devices by JAX's collectives and lax.ppermute only.
A program may use at most 640 MiB of HBM per device.

v0:
```python
import math
import jax
import jax.numpy as jnp
from jax import lax
from jax.sharding import PartitionSpec as P

NT_REC = 1024
PANEL = 256
STEPS = 2
BLOCK_START = 1022


def spread(value, axis, source):
    kept = jnp.where(lax.axis_index(axis) == source, value, 0).astype(value.dtype)
    return lax.psum(kept, axis)


def complex_terms(left, right):
    dims = (((0,), (1,)), ((), ()))

    def product(first, second):
        return lax.dot_general(first, second, dims, preferred_element_type=jnp.float32)

    real_part = product(left[0], right[0]) - product(left[1], right[1])
    imag_part = product(left[0], right[1]) + product(left[1], right[0])
    return (real_part, imag_part)


def body(traces, prior, bins, panels):
    sample_count, shots_local, receivers = traces.shape
    row_count = lax.axis_size("row")
    freq_count = lax.axis_size("freq")
    block_rows = receivers // row_count
    sample_index = BLOCK_START + jnp.arange(sample_count, dtype=jnp.int32)
    turn_count = bins[:, None] * sample_index[None, :] % NT_REC
    angles = 2.0 * math.pi / NT_REC * turn_count.astype(jnp.float32)
    twiddle = jnp.stack([jnp.cos(angles), -jnp.sin(angles)], axis=1).astype(jnp.bfloat16)
    blocked = traces.reshape(sample_count, shots_local, row_count, block_rows)
    transformed = jnp.einsum(
        "tsqb,fct->fqcsb", blocked, twiddle, preferred_element_type=jnp.float32
    ).astype(jnp.bfloat16)
    grouped = transformed.reshape(freq_count * row_count, 2, shots_local, block_rows)
    arrived = lax.all_to_all(grouped, ("freq", "row"), split_axis=0, concat_axis=2, tiled=True)
    arrived = arrived.reshape(2, freq_count * row_count * shots_local, block_rows)
    spectrum = (prior[0].astype(jnp.float32) + arrived.astype(jnp.float32)).astype(jnp.bfloat16)
    panels_each = block_rows // PANEL
    real_sum = jnp.zeros((block_rows, receivers), jnp.float32)
    imag_sum = jnp.zeros((block_rows, receivers), jnp.float32)
    for panel_step in range(STEPS):
        chosen = panels[panel_step]
        owner = chosen // panels_each
        offset = chosen % panels_each * PANEL
        own_rows = lax.dynamic_slice_in_dim(spectrum, offset, PANEL, 2)
        panel_data = spread(own_rows, "row", owner)
        left = lax.dynamic_slice_in_dim(spectrum, chosen * PANEL, PANEL, 1)
        real_part, imag_part = complex_terms(left, panel_data)
        real_sum = real_sum + real_part
        imag_sum = imag_sum + imag_part
    return (jnp.stack([real_sum, imag_sum])[None].astype(jnp.bfloat16), spectrum[None])


def solution(mesh):
    return jax.shard_map(
        body,
        mesh=mesh,
        in_specs=(P(None, ("freq", "row"), None), P("freq", None, None, "row"), P(), P()),
        out_specs=(P("freq", None, "row", None), P("freq", None, None, "row")),
        check_vma=False,
    )
```

profile of v0, /device:TPU:0, one launch (start us, length us, event | category | flops | bytes accessed | tf_op | source)
XLA Modules:
  0.0 1675.5 jit_solution(10062186824207716788)
XLA Ops:
  7.2 16.5 copy.14
  23.7 0.8 cosine_convert_fusion
  24.5 23.8 %convert_bitcast_fusion.2 = bf16[4,8,2,256,1024]{4,0,1,3,2:T(4,128)(2,1)} fusion(bf16[2,256,8,1024]{3,2,1,0:T(8,128)(2,1)} %bitcast.93, bf16[4,1,2]{0,2,1:T(2,128)(2,1)S(1)} %get-tuple-element.7, bf16[4,1,2]{0,2,1:T(2,128)(2,1)S(1)} %get-tuple-element.6), kind=kOutput, calls=%fused_computation.9 | convolution fusion | flops 83886144 | bytes 41943072 | tf_op jit(solution)/shard_map/tsqb,fct->fqcsb/dot_general | solution.py:39
  48.2 23.3 %copy.10 = bf16[4,8,2,256,1024]{4,3,2,1,0:T(8,128)(2,1)} copy(bf16[4,8,2,256,1024]{4,0,1,3,2:T(4,128)(2,1)} %convert_bitcast_fusion.2) | data formatting | bytes 67108864 | tf_op jit(solution)/shard_map/convert_element_type | solution.py:41
  71.6 0.0 copy-start
  71.6 7.4 all-to-all-start
  79.0 0.0 all-reduce.3.cloned.1.call-start
  79.0 0.0 copy-done
  79.1 0.6 fusion.27
  84.8 720.9 %all-to-all-done = bf16[32,2,256,1024]{3,2,1,0:T(8,128)(2,1)} async-done(((bf16[32,2,256,1024]{3,2,1,0:T(8,128)(2,1)}), bf16[32,2,256,1024]{3,2,1,0:T(8,128)(2,1)}, u32[]{:S(2)}, u32[]{:S(2)}) %all-to-all-start) | async-done | bytes 33554464 | tf_op jit(solution)/shard_map/all_to_all | solution.py:43
  805.7 32.3 %convert_bitcast_fusion.1 = f32[1,2,32,256,1024]{4,3,1,2,0:T(8,128)} fusion(bf16[32,2,256,1024]{3,2,1,0:T(8,128)(2,1)} %all-to-all-done), kind=kLoop, calls=%fused_computation.5 | loop fusion | flops 16777216 | bytes 100663296 | tf_op jit(solution)/shard_map/convert_element_type | solution.py:45
  838.0 43.7 %copy.11 = f32[1,2,32,256,1024]{4,3,2,1,0:T(8,128)} copy(f32[1,2,32,256,1024]{4,3,1,2,0:T(8,128)} %convert_bitcast_fusion.1) | data formatting | bytes 134217728 | tf_op jit(solution)/shard_map/convert_element_type | solution.py:45
  881.7 42.7 %fusion.1 = bf16[2,8192,1024]{2,1,0:T(8,128)(2,1)} fusion(f32[2,8192,1024]{2,1,0:T(8,128)} %bitcast.8, bf16[1,2,8192,1024]{3,2,1,0:T(8,128)(2,1)} %param.5), kind=kLoop, calls=%fused_computation.3 | loop fusion | flops 50331648 | bytes 134217728 | tf_op jit(solution)/shard_map/convert_element_type | solution.py:45
  924.3 12.3 dynamic-slice_select_fusion.1
  936.6 0.0 all-reduce.3.cloned.1.call-update
  937.9 43.1 %fusion.2 = bf16[1,2,8192,1024]{3,2,1,0:T(8,128)(2,1)} fusion(bf16[1,2,8192,1024]{3,2,1,0:T(8,128)(2,1)} %param.5, f32[1,2,32,256,1024]{4,3,2,1,0:T(8,128)} %copy.11), kind=kLoop, calls=%fused_computation.4 | loop fusion | flops 50331648 | bytes 134217728 | tf_op jit(solution)/shard_map/convert_element_type | solution.py:45
  981.0 492.7 %all-reduce.3.cloned.1.call-done = (bf16[2,8192,256]{2,1,0:T(8,128)(2,1)}, bf16[2,8192,256]{2,1,0:T(8,128)(2,1)}) async-done(((bf16[2,8192,256]{2,1,0:T(8,128)(2,1)}, bf16[2,8192,256]{2,1,0:T(8,128)(2,1)}), (bf16[2,8192,256]{2,1,0:T(8,128)(2,1)}, bf16[2,8192,256]{2,1,0:T(8,128)(2,1)})) %all-reduce.3.cloned.1.call-update) | async-done | bytes 16777232 | tf_op jit(solution)/shard_map/psum | solution.py:15
  1473.7 0.0 slice-start
  1473.7 0.0 slice-start.1
  1473.7 18.2 %fusion.12 = f32[1024,8192]{1,0:T(8,128)} fusion(bf16[2,8192,256]{2,1,0:T(8,128)(2,1)} %get-tuple-element.2, bf16[2,8192,1024]{2,1,0:T(8,128)(2,1)} %fusion.1, s32[]{:T(128)S(6)} %select_n.68), kind=kOutput, calls=%fused_computation.25 | convolution fusion | flops 4294967296 | bytes 38273028 | tf_op jit(solution)/shard_map/dot_general | solution.py:22
  1491.9 0.0 slice-done
  1491.9 0.0 slice-done.1
  1491.9 14.3 fusion.11
  1506.2 0.0 slice-start.2
  1506.2 0.0 slice-start.3
  1506.2 18.2 %fusion.9 = f32[1024,8192]{1,0:T(8,128)} fusion(bf16[2,8192,256]{2,1,0:T(8,128)(2,1)} %get-tuple-element.3, bf16[2,8192,1024]{2,1,0:T(8,128)(2,1)} %fusion.1, s32[]{:T(128)S(6)} %select_n.62), kind=kOutput, calls=%fused_computation.22 | convolution fusion | flops 4294967296 | bytes 38273028 | tf_op jit(solution)/shard_map/dot_general | solution.py:22
  1524.4 0.0 slice-done.2
  1524.4 0.0 slice-done.3
  1524.4 14.2 fusion.7
  1538.6 14.2 fusion.10
  1552.8 14.4 fusion.8
  1567.2 39.1 %fusion.4 = bf16[1,1,1024,8192]{3,2,1,0:T(8,128)(2,1)} fusion(f32[1024,8192]{1,0:T(8,128)} %fusion.12, f32[1024,8192]{1,0:T(8,128)} %fusion.9, f32[1024,8192]{1,0:T(8,128)} %fusion.7, bf16[2,8192,256]{2,1,0:T(8,128)(2,1)} %get-tuple-element.2, bf16[2,8192,1024]{2,1,0:T(8,128)(2,1)} %fusion.1, s32[]{:T(128)S(6)} %add.81, s32[]{:T(128)S(6)} %select_n.68), kind=kOutput, calls=%fused_computation.11 | convolution fusion | flops 4328521728 | bytes 122159112 | tf_op jit(solution)/shard_map/dot_general | solution.py:22
  1606.3 39.1 %fusion.3 = bf16[1,1,1024,8192]{3,2,1,0:T(8,128)(2,1)} fusion(f32[1024,8192]{1,0:T(8,128)} %fusion.11, f32[1024,8192]{1,0:T(8,128)} %fusion.8, f32[1024,8192]{1,0:T(8,128)} %fusion.10, bf16[2,8192,256]{2,1,0:T(8,128)(2,1)} %get-tuple-element.2, bf16[2,8192,1024]{2,1,0:T(8,128)(2,1)} %fusion.1, s32[]{:T(128)S(6)} %add.81, s32[]{:T(128)S(6)} %select_n.68), kind=kOutput, calls=%fused_computation.10 | convolution fusion | flops 4328521728 | bytes 122159112 | tf_op jit(solution)/shard_map/dot_general | solution.py:22
  1645.5 23.0 %pad_maximum_fusion = bf16[1,2,1024,8192]{3,2,1,0:T(8,128)(2,1)} fusion(bf16[1,1,1024,8192]{3,2,1,0:T(8,128)(2,1)} %fusion.4, bf16[1,1,1024,8192]{3,2,1,0:T(8,128)(2,1)} %fusion.3), kind=kLoop, calls=%fused_computation.6 | loop fusion | flops 16777216 | bytes 67108864 | tf_op jit(solution)/shard_map/stack | solution.py:59
  (3 shorter events, 0.0 us)
Async XLA Ops:
  71.6 7.5 copy-start
  71.6 734.1 %all-to-all-start = ((bf16[32,2,256,1024]{3,2,1,0:T(8,128)(2,1)}), bf16[32,2,256,1024]{3,2,1,0:T(8,128)(2,1)}, u32[]{:S(2)}, u32[]{:S(2)}) async-start(bf16[32,2,256,1024]{3,2,1,0:T(8,128)(2,1)} %bitcast.87), calls=%async_computation | async-start | bytes 67108864 | tf_op jit(solution)/shard_map/all_to_all | solution.py:43
  79.0 1394.7 %all-reduce.3.cloned.1.call-start = ((), (), s32[]{:S(2)}) async-start(), calls=%async_computation.1 | async-start | bytes 33554432 | tf_op jit(solution)/shard_map/psum | solution.py:15
  1473.7 18.2 %slice-start = ((s8[8388608]{0:T(1024)(128)(4,1)}), s8[4194304]{0:T(1024)(128)(4,1)S(1)}, s32[]{:S(2)}) async-start(s8[8388608]{0:T(1024)(128)(4,1)} %bitcast.88), calls=%async_computation.2 | async-start | bytes 8388608
  1473.7 18.2 %slice-start.1 = ((s8[8388608]{0:T(1024)(128)(4,1)}), s8[4194304]{0:T(1024)(128)(4,1)S(1)}, s32[]{:S(2)}) async-start(s8[8388608]{0:T(1024)(128)(4,1)} %bitcast.88), calls=%async_computation.3 | async-start | bytes 8388608
  1506.2 18.2 %slice-start.2 = ((s8[8388608]{0:T(1024)(128)(4,1)}), s8[4194304]{0:T(1024)(128)(4,1)S(1)}, s32[]{:S(2)}) async-start(s8[8388608]{0:T(1024)(128)(4,1)} %bitcast.90), calls=%async_computation.4 | async-start | bytes 8388608
  1506.2 18.2 %slice-start.3 = ((s8[8388608]{0:T(1024)(128)(4,1)}), s8[4194304]{0:T(1024)(128)(4,1)S(1)}, s32[]{:S(2)}) async-start(s8[8388608]{0:T(1024)(128)(4,1)} %bitcast.90), calls=%async_computation.5 | async-start | bytes 8388608
Sparse Core Ops, SparseCore 0:
  936.8 536.8 all-reduce.2
where the time goes:
time: 1680 us
  waiting for transfers between devices  1210 us (72%)
  matrix products  195 us (12%)
  other arithmetic  154 us (9%)
  local copies, waits for them, and re-layouts  84.2 us (5%)
  between operations  20.7 us (1%)
    all_to_all x1, waiting for transfers between devices, body(): lax.all_to_all(grouped, ('freq', 'row'), split_axis=0, concat_axis=2, til...  721 us
    psum x1, waiting for transfers between devices, spread(): return lax.psum(kept, axis)  493 us
    dot_general x8, matrix products, product(): lax.dot_general(first, second, dims, preferred_element_type=jnp.float32)  172 us
    convert_element_type x2, other arithmetic, body(): (prior[0].astype(jnp.float32) + arrived.astype(jnp.float32)).astype(jnp.b...  85.7 us
    convert_element_type x1, local copies, waits for them, and re-layouts, body(): arrived.astype(jnp.float32)  43.7 us
  transfers between devices with their start and end apart: 2, of which 2 were waited for; matrix products, arithmetic and copies ran while one was open for 3% of the time, Pallas kernels for 0%

commit v1 on v0

--- a/solution.py
+++ b/solution.py
@@ -8,6 +8,12 @@
 PANEL = 256
 STEPS = 2
 BLOCK_START = 1022
+
+
+def stacked_exchange(x, name, split, join):
+    shards = jnp.split(x, lax.axis_size(name), axis=split)
+    got = lax.all_to_all(jnp.stack(shards), name, 0, 0)
+    return jnp.concatenate(got, axis=join)
 
 
 def spread(value, axis, source):
@@ -40,7 +46,7 @@
         "tsqb,fct->fqcsb", blocked, twiddle, preferred_element_type=jnp.float32
     ).astype(jnp.bfloat16)
     grouped = transformed.reshape(freq_count * row_count, 2, shots_local, block_rows)
-    arrived = lax.all_to_all(grouped, ("freq", "row"), split_axis=0, concat_axis=2, tiled=True)
+    arrived = stacked_exchange(grouped, ("freq", "row"), 0, 2)
     arrived = arrived.reshape(2, freq_count * row_count * shots_local, block_rows)
     spectrum = (prior[0].astype(jnp.float32) + arrived.astype(jnp.float32)).astype(jnp.bfloat16)
     panels_each = block_rows // PANEL

time: 1680 us -> 1740 us (1.036)
  local copies, waits for them, and re-layouts: 84.2 us -> 140 us
    unnamed x11 -> x44, local copies, waits for them, and re-layouts: 16.5 us -> 71.4 us
where the time goes in v1:
time: 1740 us; the launch traced here: 1730 us
  waiting for transfers between devices  1210 us (70%)
  matrix products  195 us (11%)
  other arithmetic  154 us (9%)
  local copies, waits for them, and re-layouts  140 us (8%)
  between operations  20.9 us (1%)
    all_to_all x1, waiting for transfers between devices, stacked_exchange(): got = lax.all_to_all(jnp.stack(shards), name, 0, 0)  721 us
    psum x1, waiting for transfers between devices, spread(): return lax.psum(kept, axis)  493 us
    dot_general x8, matrix products, product(): lax.dot_general(first, second, dims, preferred_element_type=jnp.float32)  171 us
    convert_element_type x2, other arithmetic, body(): (prior[0].astype(jnp.float32) + arrived.astype(jnp.float32)).astype(jnp.b...  85.7 us
    unnamed x44, local copies, waits for them, and re-layouts  71.4 us
    convert_element_type x1, local copies, waits for them, and re-layouts, body(): arrived.astype(jnp.float32)  43.7 us
  transfers between devices with their start and end apart: 2, of which 2 were waited for; matrix products, arithmetic and copies ran while one was open for 3% of the time, Pallas kernels for 0%

profile of v1, /device:TPU:0, one launch (start us, length us, event | category | flops | bytes accessed | tf_op | source)
XLA Modules:
  0.0 1731.6 jit_solution(13340839344358983628)
XLA Ops:
  7.2 16.5 copy.45
  24.5 23.8 %convert_bitcast_fusion.2 = bf16[4,8,2,256,1024]{4,0,1,3,2:T(4,128)(2,1)} fusion(bf16[2,256,8,1024]{3,2,1,0:T(8,128)(2,1)} %bitcast.249, bf16[4,1,2]{0,2,1:T(2,128)(2,1)S(1)} %get-tuple-element.7, bf16[4,1,2]{0,2,1:T(2,128)(2,1)S(1)} %get-tuple-element.6), kind=kOutput, calls=%fused_computation.9 | convolution fusion | flops 83886144 | bytes 41943072 | tf_op jit(solution)/shard_map/tsqb,fct->fqcsb/dot_general | solution.py:45
  48.3 23.3 %copy.41 = bf16[4,8,2,256,1024]{4,3,2,1,0:T(8,128)(2,1)} copy(bf16[4,8,2,256,1024]{4,0,1,3,2:T(4,128)(2,1)} %convert_bitcast_fusion.2) | data formatting | bytes 67108864 | tf_op jit(solution)/shard_map/convert_element_type | solution.py:47
  71.6 2.4 fusion.44
  74.0 3.0 fusion.43
  77.0 3.0 fusion.42
  80.1 3.0 fusion.41
  83.1 3.0 fusion.40
  86.1 2.3 fusion.39
  88.3 2.3 fusion.38
  90.6 2.3 fusion.37
  92.9 2.3 fusion.36
  95.1 2.3 fusion.35
  97.4 2.3 fusion.34
  99.6 2.3 fusion.33
  101.9 2.3 fusion.32
  104.2 2.3 fusion.31
  106.4 2.3 fusion.30
  108.7 2.3 fusion.29
  111.0 1.0 fusion.28
  116.1 1.0 fusion.23
  117.2 1.0 fusion.22
  118.2 1.0 fusion.21
  119.3 1.0 fusion.20
  120.3 1.0 fusion.19
  121.3 1.0 fusion.18
  122.4 1.0 fusion.17
  123.4 1.0 fusion.16
  124.5 1.0 fusion.15
  125.5 1.0 fusion.14
  126.5 1.0 fusion.13
  127.6 7.4 all-to-all-start
  140.8 720.9 %all-to-all-done = bf16[32,1,2,256,1024]{4,3,2,1,0:T(8,128)(2,1)} async-done(((bf16[32,1,2,256,1024]{4,3,2,1,0:T(8,128)(2,1)}), bf16[32,1,2,256,1024]{4,3,2,1,0:T(8,128)(2,1)}, u32[]{:S(2)}, u32[]{:S(2)}) %all-to-all-start) | async-done | bytes 33554464 | tf_op jit(solution)/shard_map/all_to_all | solution.py:15
  861.7 32.5 %convert_bitcast_fusion.1 = f32[1,2,32,256,1024]{4,3,1,0,2:T(8,128)} fusion(bf16[32,1,2,256,1024]{4,3,2,1,0:T(8,128)(2,1)} %all-to-all-done), kind=kLoop, calls=%fused_computation.5 | loop fusion | flops 16777216 | bytes 100663296 | tf_op jit(solution)/shard_map/convert_element_type | solution.py:51
  894.1 43.7 %copy.42 = f32[1,2,32,256,1024]{4,3,2,1,0:T(8,128)} copy(f32[1,2,32,256,1024]{4,3,1,0,2:T(8,128)} %convert_bitcast_fusion.1) | data formatting | bytes 134217728 | tf_op jit(solution)/shard_map/convert_element_type | solution.py:51
  937.9 42.7 %fusion.1 = bf16[2,8192,1024]{2,1,0:T(8,128)(2,1)} fusion(f32[2,8192,1024]{2,1,0:T(8,128)} %bitcast.39, bf16[1,2,8192,1024]{3,2,1,0:T(8,128)(2,1)} %param.5), kind=kLoop, calls=%fused_computation.3 | loop fusion | flops 50331648 | bytes 134217728 | tf_op jit(solution)/shard_map/convert_element_type | solution.py:51
  980.5 12.3 dynamic-slice_select_fusion.1
  994.1 43.1 %fusion.2 = bf16[1,2,8192,1024]{3,2,1,0:T(8,128)(2,1)} fusion(bf16[1,2,8192,1024]{3,2,1,0:T(8,128)(2,1)} %param.5, f32[1,2,32,256,1024]{4,3,2,1,0:T(8,128)} %copy.42), kind=kLoop, calls=%fused_computation.4 | loop fusion | flops 50331648 | bytes 134217728 | tf_op jit(solution)/shard_map/convert_element_type | solution.py:51
  1037.2 492.7 %all-reduce.3.cloned.1.call-done = (bf16[2,8192,256]{2,1,0:T(8,128)(2,1)}, bf16[2,8192,256]{2,1,0:T(8,128)(2,1)}) async-done(((bf16[2,8192,256]{2,1,0:T(8,128)(2,1)}, bf16[2,8192,256]{2,1,0:T(8,128)(2,1)}), (bf16[2,8192,256]{2,1,0:T(8,128)(2,1)}, bf16[2,8192,256]{2,1,0:T(8,128)(2,1)})) %all-reduce.3.cloned.1.call-update) | async-done | bytes 16777232 | tf_op jit(solution)/shard_map/psum | solution.py:21
  1529.9 18.2 %fusion.12 = f32[1024,8192]{1,0:T(8,128)} fusion(bf16[2,8192,256]{2,1,0:T(8,128)(2,1)} %get-tuple-element.2, bf16[2,8192,1024]{2,1,0:T(8,128)(2,1)} %fusion.1, s32[]{:T(128)S(6)} %select_n.68), kind=kOutput, calls=%fused_computation.25 | convolution fusion | flops 4294967296 | bytes 38273028 | tf_op jit(solution)/shard_map/dot_general | solution.py:28
  1548.1 14.4 fusion.11
  1562.4 18.2 %fusion.9 = f32[1024,8192]{1,0:T(8,128)} fusion(bf16[2,8192,256]{2,1,0:T(8,128)(2,1)} %get-tuple-element.3, bf16[2,8192,1024]{2,1,0:T(8,128)(2,1)} %fusion.1, s32[]{:T(128)S(6)} %select_n.62), kind=kOutput, calls=%fused_computation.22 | convolution fusion | flops 4294967296 | bytes 38273028 | tf_op jit(solution)/shard_map/dot_general | solution.py:28
  1580.6 14.2 fusion.7
  1594.8 14.2 fusion.10
  1608.9 14.4 fusion.8
  1623.3 39.0 %fusion.4 = bf16[1,1,1024,8192]{3,2,1,0:T(8,128)(2,1)} fusion(f32[1024,8192]{1,0:T(8,128)} %fusion.12, f32[1024,8192]{1,0:T(8,128)} %fusion.9, f32[1024,8192]{1,0:T(8,128)} %fusion.7, bf16[2,8192,256]{2,1,0:T(8,128)(2,1)} %get-tuple-element.2, bf16[2,8192,1024]{2,1,0:T(8,128)(2,1)} %fusion.1, s32[]{:T(128)S(6)} %add.81, s32[]{:T(128)S(6)} %select_n.68), kind=kOutput, calls=%fused_computation.11 | convolution fusion | flops 4328521728 | bytes 122159112 | tf_op jit(solution)/shard_map/dot_general | solution.py:28
  1662.4 39.0 %fusion.3 = bf16[1,1,1024,8192]{3,2,1,0:T(8,128)(2,1)} fusion(f32[1024,8192]{1,0:T(8,128)} %fusion.11, f32[1024,8192]{1,0:T(8,128)} %fusion.8, f32[1024,8192]{1,0:T(8,128)} %fusion.10, bf16[2,8192,256]{2,1,0:T(8,128)(2,1)} %get-tuple-element.2, bf16[2,8192,1024]{2,1,0:T(8,128)(2,1)} %fusion.1, s32[]{:T(128)S(6)} %add.81, s32[]{:T(128)S(6)} %select_n.68), kind=kOutput, calls=%fused_computation.10 | convolution fusion | flops 4328521728 | bytes 122159112 | tf_op jit(solution)/shard_map/dot_general | solution.py:28
  1701.4 23.0 %pad_maximum_fusion = bf16[1,2,1024,8192]{3,2,1,0:T(8,128)(2,1)} fusion(bf16[1,1,1024,8192]{3,2,1,0:T(8,128)(2,1)} %fusion.4, bf16[1,1,1024,8192]{3,2,1,0:T(8,128)(2,1)} %fusion.3), kind=kLoop, calls=%fused_computation.6 | loop fusion | flops 16777216 | bytes 67108864 | tf_op jit(solution)/shard_map/stack | solution.py:65
  (23 shorter events, 5.7 us)
Async XLA Ops:
  71.6 39.3 %copy-start = (bf16[4,8,2,256,1024]{4,3,2,1,0:T(8,128)(2,1)S(1)}, bf16[4,8,2,256,1024]{4,3,2,1,0:T(8,128)(2,1)}, u32[]{:S(2)}) copy-start(bf16[4,8,2,256,1024]{4,3,2,1,0:T(8,128)(2,1)} %copy.41) | copy-start | bytes 100663296
  127.6 7.5 copy-start.1
  127.6 734.1 %all-to-all-start = ((bf16[32,1,2,256,1024]{4,3,2,1,0:T(8,128)(2,1)}), bf16[32,1,2,256,1024]{4,3,2,1,0:T(8,128)(2,1)}, u32[]{:S(2)}, u32[]{:S(2)}) async-start(bf16[32,1,2,256,1024]{4,3,2,1,0:T(8,128)(2,1)} %fusion.13), calls=%async_computation | async-start | bytes 67108864 | tf_op jit(solution)/shard_map/all_to_all | solution.py:15
  135.0 1394.9 %all-reduce.3.cloned.1.call-start = ((), (), s32[]{:S(2)}) async-start(), calls=%async_computation.1 | async-start | bytes 33554432 | tf_op jit(solution)/shard_map/psum | solution.py:21
  1529.9 18.2 %slice-start = ((s8[8388608]{0:T(1024)(128)(4,1)}), s8[4194304]{0:T(1024)(128)(4,1)S(1)}, s32[]{:S(2)}) async-start(s8[8388608]{0:T(1024)(128)(4,1)} %bitcast.244), calls=%async_computation.2 | async-start | bytes 8388608
  1529.9 18.2 %slice-start.1 = ((s8[8388608]{0:T(1024)(128)(4,1)}), s8[4194304]{0:T(1024)(128)(4,1)S(1)}, s32[]{:S(2)}) async-start(s8[8388608]{0:T(1024)(128)(4,1)} %bitcast.244), calls=%async_computation.3 | async-start | bytes 8388608
  1562.4 18.2 %slice-start.2 = ((s8[8388608]{0:T(1024)(128)(4,1)}), s8[4194304]{0:T(1024)(128)(4,1)S(1)}, s32[]{:S(2)}) async-start(s8[8388608]{0:T(1024)(128)(4,1)} %bitcast.246), calls=%async_computation.4 | async-start | bytes 8388608
  1562.4 18.2 %slice-start.3 = ((s8[8388608]{0:T(1024)(128)(4,1)}), s8[4194304]{0:T(1024)(128)(4,1)S(1)}, s32[]{:S(2)}) async-start(s8[8388608]{0:T(1024)(128)(4,1)} %bitcast.246), calls=%async_computation.5 | async-start | bytes 8388608
Sparse Core Ops, SparseCore 0:
  993.0 536.8 all-reduce.2
